TPU v7x, 128 devices: a whole 4x4x4 slice. The times are simulated.
128 devices in a mesh: grp: 8 (over x_hi, z), vocab: 16 (over y, x_lo, core).
Axes of the slice: x: 4 (x_hi: 2, x_lo: 2; x = x_hi * 2 + x_lo), y: 4, z: 4, core: 2. Of those that a mesh axis runs over, the one named last changes fastest.
Arguments:
- hidden: bfloat16 [1024, 8192], P('grp', 'vocab')
- head_weight: bfloat16 [81920, 8192], P(('grp', 'vocab'))
- targets: int32 [1024], replicated, may hold values from 0 to 81919
- old_logprobs: float32 [1024], replicated
- loss_mask: int32 [1024], replicated, may hold values 0 or 1
- beam_lengths: int32 [128], replicated, may hold values from 1 to 24, 1024 in all
- beam_group: int32 [128], replicated, may hold values from 0 to 1, as said below
- rewards: float32 [128], replicated, may hold values from 0 to 1, as said below
Outputs:
- logprob: float32 [1024], replicated
- total_loss: float32 [], replicated
- head_grad: bfloat16 [81920, 8192], P(('grp', 'vocab'))
Inputs may be any that keep to these rules, and one draw needn't show every extreme that they name: `beam_group`: each of the 2 groups is named by exactly 64 beams. `rewards`: multiples of 1/8.
All inputs are finite; a program needn't handle non-finite values.
Results may differ from a plain program's by a relative error of at most 0.005.
Values may be sent and summed in bfloat16 or wider, within the bound.
No kernel may reach another device: no remote copies, remote signals or barrier semaphores. Data moves between devices by JAX's collectives and lax.ppermute only.
A program may use at most 128 MiB of HBM per device.

v0:
```python
import jax
import jax.numpy as jnp
from jax import lax
from jax.sharding import PartitionSpec as P

GROUP_BEAMS = 64


def policy_terms(logprob, old_logprobs, loss_mask, beam_lengths, beam_group, rewards):
    highest = lax.Precision.HIGHEST
    tok_count = logprob.shape[0]
    beam_count = beam_lengths.shape[0]
    group_count = beam_count // GROUP_BEAMS
    beam_ends = jnp.cumsum(beam_lengths)
    position = jnp.arange(tok_count, dtype=jnp.int32)
    beam_of = jnp.sum((position[:, None] >= beam_ends[None, :]).astype(jnp.int32), axis=1)
    token_beam = (beam_of[:, None] == jnp.arange(beam_count, dtype=jnp.int32)[None, :]).astype(
        jnp.float32
    )
    beam_onehot = (beam_group[:, None] == jnp.arange(group_count, dtype=jnp.int32)[None, :]).astype(
        jnp.float32
    )
    group_mean = jnp.dot(rewards, beam_onehot, precision=highest) / GROUP_BEAMS
    centred = rewards - jnp.dot(beam_onehot, group_mean, precision=highest)
    group_var = jnp.dot(centred * centred, beam_onehot, precision=highest) / GROUP_BEAMS
    advantage = centred / jnp.sqrt(jnp.dot(beam_onehot, group_var, precision=highest) + 1e-06)
    weight = loss_mask.astype(jnp.float32)
    counts = jnp.dot(weight, token_beam, precision=highest)
    token_adv = jnp.dot(token_beam, advantage, precision=highest)
    token_norm = jnp.dot(token_beam, jnp.maximum(counts, 1.0), precision=highest)
    ratios = jnp.exp(logprob - old_logprobs)
    clipped = jnp.clip(ratios, 0.8, 1.2)
    plain_term = ratios * token_adv
    bounded = clipped * token_adv
    token_share = weight / token_norm
    total_loss = -jnp.sum(token_share * jnp.minimum(plain_term, bounded))
    slopes = -token_share * jnp.where(plain_term <= bounded, plain_term, 0.0)
    return (total_loss, slopes)


def shards(
    hidden, head_weight, targets, old_logprobs, loss_mask, beam_lengths, beam_group, rewards
):
    token_block = lax.all_gather(hidden, "grp", axis=0, tiled=True)
    features = lax.all_gather(token_block, "vocab", axis=1, tiled=True)
    shard = head_weight.shape[0]
    offset = (lax.axis_index("grp") * lax.axis_size("vocab") + lax.axis_index("vocab")) * shard
    vocab_ids = offset + jnp.arange(shard, dtype=jnp.int32)
    logits = lax.dot_general(
        features, head_weight, (((1,), (1,)), ((), ())), preferred_element_type=jnp.float32
    )
    hits = targets[:, None] == vocab_ids[None, :]
    picked = jnp.sum(jnp.where(hits, logits, 0.0), axis=1)
    top = lax.pmax(jnp.max(logits, axis=1), ("grp", "vocab"))
    local_sum = jnp.sum(jnp.exp(logits - top[:, None]), axis=1)
    total, target_logit = lax.psum((local_sum, picked), ("grp", "vocab"))
    log_total = top + jnp.log(total)
    logprob = target_logit - log_total
    total_loss, slopes = policy_terms(
        logprob, old_logprobs, loss_mask, beam_lengths, beam_group, rewards
    )
    grads = (
        slopes[:, None] * (hits.astype(jnp.float32) - jnp.exp(logits - log_total[:, None]))
    ).astype(jnp.bfloat16)
    head_grad = lax.dot_general(
        grads, features, (((0,), (0,)), ((), ())), preferred_element_type=jnp.float32
    )
    return (logprob, total_loss, head_grad.astype(jnp.bfloat16))


def solution(mesh):
    in_specs = (P("grp", "vocab"), P(("grp", "vocab"), None), P(), P(), P(), P(), P(), P())
    out_specs = (P(), P(), P(("grp", "vocab"), None))
    return jax.shard_map(shards, mesh=mesh, in_specs=in_specs, out_specs=out_specs, check_vma=False)
```

profile of v0, /device:TPU:0, one launch (start us, length us, event | category | flops | bytes accessed | tf_op | source)
XLA Modules:
  0.0 326.3 jit_solution(1257413996547602422)
XLA Ops:
  7.2 0.0 all-gather.3.cloned.1.call-start
  7.2 0.7 all-gather.3.cloned.1.call-update
  7.9 0.0 all-gather.5.cloned.1.call-start
  7.9 51.4 %all-gather.3.cloned.1.call-done = bf16[1024,512]{1,0:T(8,128)(2,1)} async-done(((bf16[128,512]{1,0:T(8,128)(2,1)}), bf16[1024,512]{1,0:T(8,128)(2,1)}) %all-gather.3.cloned.1.call-update) | async-done | bytes 1048592 | tf_op jit(solution)/shard_map/all_gather | solution.py:44
  59.3 0.0 all-gather.5.cloned.1.call-update
  59.3 0.7 convert_element_type.17
  60.0 0.8 copy.13
  60.8 0.2 reduce-window.8
  60.9 0.1 reduce
  61.1 0.9 fusion.15
  61.9 1.0 fusion.13
  62.9 0.9 fusion.12
  63.8 0.9 fusion.17
  64.7 0.2 convert_reduce_fusion
  64.9 0.4 fusion.19
  65.3 0.5 fusion.21
  65.8 0.4 fusion.20
  66.2 0.0 copy-start.3
  66.2 85.1 %all-gather.5.cloned.1.call-done = bf16[1024,8192]{1,0:T(8,128)(2,1)} async-done(((bf16[1024,512]{1,0:T(8,128)(2,1)}), bf16[1024,8192]{1,0:T(8,128)(2,1)}) %all-gather.5.cloned.1.call-update) | async-done | bytes 16777232 | tf_op jit(solution)/shard_map/all_gather | solution.py:45
  151.3 16.3 %fusion.33 = (f32[1024]{0:T(1024)S(1)}, f32[1024,640]{0,1:T(8,128)S(1)}) fusion(bf16[1024,8192]{1,0:T(8,128)(2,1)} %all-gather.5.cloned.1.call-done, bf16[640,8192]{1,0:T(8,128)(2,1)} %param.9), kind=kOutput, calls=%fused_computation.52 | convolution fusion | flops 10738072576 | bytes 29888512 | tf_op jit(solution)/shard_map/dot_general | solution.py:49
  167.6 0.0 copy-start
  167.6 0.0 copy-start.1
  167.6 66.5 %pmax.7 = f32[1024]{0:T(1024)S(1)} all-reduce(f32[1024]{0:T(1024)S(1)} %get-tuple-element.10), channel_id=1, replica_groups=mesh['grp'=8,'vocab'=16] {'grp','vocab'}, use_global_device_ids=true, to_apply=%region_3.4 | all-reduce | flops 1024 | bytes 8192 | tf_op jit(solution)/shard_map/pmax | solution.py:54
  234.1 0.0 copy-done.3
  234.1 0.6 exponential_reduce_fusion
  234.7 62.8 %all-reduce = (f32[1024]{0:T(1024)S(1)}, f32[1024]{0:T(1024)S(1)}) all-reduce(f32[1024]{0:T(1024)S(1)} %get-tuple-element.4, f32[1024]{0:T(1024)S(1)} %get-tuple-element.3), channel_id=1, replica_groups=mesh['grp'=8,'vocab'=16] {'grp','vocab'}, use_global_device_ids=true, to_apply=%region_1.2 | all-reduce | flops 2048 | bytes 16384 | tf_op jit(solution)/shard_map/psum | solution.py:56
  297.5 0.0 copy-done
  297.5 0.0 copy-done.1
  297.5 0.0 copy-start.2
  297.5 0.6 multiply_reduce_fusion
  298.8 19.5 %convolution_convert_fusion = bf16[640,8192]{1,0:T(8,128)(2,1)} fusion(bf16[1024,8192]{1,0:T(8,128)(2,1)} %all-gather.5.cloned.1.call-done, f32[1024,640]{0,1:T(8,128)S(1)} %get-tuple-element.11, f32[1024]{0:T(1024)S(1)} %get-tuple-element.9, f32[1024]{0:T(1024)S(1)} %get-tuple-element.7, s32[1024]{0:T(1024)S(1)} %copy-done.3, s32[640]{0:T(1024)S(1)} %iota_add_fusion), kind=kOutput, calls=%fused_computation | convolution fusion | flops 10746593280 | bytes 29899264 | tf_op jit(solution)/shard_map/dot_general | solution.py:65
  318.3 0.0 copy-done.2
  (2 shorter events, 0.0 us)
Async XLA Ops:
  7.2 52.1 %all-gather.3.cloned.1.call-start = ((), (), s32[]{:S(2)}) async-start(), calls=%async_computation | async-start | bytes 1179648 | tf_op jit(solution)/shard_map/all_gather | solution.py:44
  7.9 143.4 %all-gather.5.cloned.1.call-start = ((), (), s32[]{:S(2)}) async-start(), calls=%async_computation.1 | async-start | bytes 17825792 | tf_op jit(solution)/shard_map/all_gather | solution.py:45
  66.2 167.9 %copy-start.3 = (s32[1024]{0:T(1024)S(1)}, s32[1024]{0:T(1024)}, u32[]{:S(2)}) copy-start(s32[1024]{0:T(1024)} %param.10) | copy-start | bytes 12292
  167.6 129.9 %copy-start = (s32[1024]{0:T(1024)S(1)}, s32[1024]{0:T(1024)}, u32[]{:S(2)}) copy-start(s32[1024]{0:T(1024)} %param.12) | copy-start | bytes 12292
  167.6 129.9 %copy-start.1 = (f32[1024]{0:T(1024)S(1)}, f32[1024]{0:T(1024)}, u32[]{:S(2)}) copy-start(f32[1024]{0:T(1024)} %param.11) | copy-start | bytes 12292
  297.5 20.8 %copy-start.2 = (f32[1024]{0:T(1024)}, f32[1024]{0:T(1024)S(1)}, u32[]{:S(2)}) copy-start(f32[1024]{0:T(1024)S(1)} %get-tuple-element.8) | copy-start | bytes 12292
Sparse Core Ops, SparseCore 0:
  10.3 48.9 all-gather.2
  61.0 90.2 all-gather.4
where the time goes:
time: 328 us; the launch traced here: 326 us
  waiting for transfers between devices  137 us (42%)
  blocking collectives  129 us (39%)
  matrix products  40.7 us (12%)
  between operations  15.9 us (5%)
    all_gather x1, waiting for transfers between devices, shards(): features = lax.all_gather(token_block, 'vocab', axis=1, tiled=True)  85.1 us
    pmax x1, blocking collectives, shards(): top = lax.pmax(jnp.max(logits, axis=1), ('grp', 'vocab'))  66.5 us
    psum x1, blocking collectives, shards(): total, target_logit = lax.psum((local_sum, picked), ('grp', 'vocab'))  62.8 us
    all_gather x1, waiting for transfers between devices, shards(): token_block = lax.all_gather(hidden, 'grp', axis=0, tiled=True)  51.4 us
    dot_general x1, matrix products, shards(): lax.dot_general(grads, features, (((0,), (0,)), ((), ())), preferred_elem...  19.5 us
    dot_general x1, matrix products, shards(): lax.dot_general(features, head_weight, (((1,), (1,)), ((), ())), preferre...  16.3 us
  transfers between devices with their start and end apart: 2, of which 2 were waited for; matrix products, arithmetic and copies ran while one was open for 2% of the time, Pallas kernels for 0%

commit v1 on v0

--- a/solution.py
+++ b/solution.py
@@ -38,6 +38,23 @@
     return (total_loss, slopes)
 
 
+def combine(mine, theirs):
+    top = jnp.maximum(mine[0], theirs[0])
+    total = mine[1] * jnp.exp(mine[0] - top) + theirs[1] * jnp.exp(theirs[0] - top)
+    return jnp.stack([top, total, mine[2] + theirs[2]])
+
+
+def butterfly(stats):
+    for axis in ("vocab", "grp"):
+        size = lax.axis_size(axis)
+        step = 1
+        while step < size:
+            perm = [(i, i ^ step) for i in range(size)]
+            stats = combine(stats, lax.ppermute(stats, axis, perm))
+            step *= 2
+    return stats[0], stats[1], stats[2]
+
+
 def shards(
     hidden, head_weight, targets, old_logprobs, loss_mask, beam_lengths, beam_group, rewards
 ):
@@ -51,9 +68,9 @@
     )
     hits = targets[:, None] == vocab_ids[None, :]
     picked = jnp.sum(jnp.where(hits, logits, 0.0), axis=1)
-    top = lax.pmax(jnp.max(logits, axis=1), ("grp", "vocab"))
-    local_sum = jnp.sum(jnp.exp(logits - top[:, None]), axis=1)
-    total, target_logit = lax.psum((local_sum, picked), ("grp", "vocab"))
+    local_top = jnp.max(logits, axis=1)
+    local_sum = jnp.sum(jnp.exp(logits - local_top[:, None]), axis=1)
+    top, total, target_logit = butterfly(jnp.stack([local_top, local_sum, picked]))
     log_total = top + jnp.log(total)
     logprob = target_logit - log_total
     total_loss, slopes = policy_terms(

time: 328 us -> 227 us (0.69)
  blocking collectives: 129 us -> 0 us
  waiting for transfers between devices: 137 us -> 155 us
  starting transfers between devices: 0.08 us -> 14.3 us
    pmax x1 -> x0, blocking collectives: 66.5 us -> none  [shards(): top = lax.pmax(jnp.max(logits, axis=1), ('grp', 'vocab'))]
    psum x1 -> x0, blocking collectives: 62.8 us -> none  [shards(): total, target_logit = lax.psum((local_sum, picked), ('grp', 'vocab'))]
    ppermute x0 -> x7, starting transfers between devices: none -> 14.2 us  [butterfly(): stats = combine(stats, lax.ppermute(stats, axis, perm))]
    ppermute x0 -> x7, waiting for transfers between devices: none -> 12.7 us  [butterfly(): stats = combine(stats, lax.ppermute(stats, axis, perm))]
    all_gather x1, waiting for transfers between devices: 85.1 us -> 90 us  [shards(): features = lax.all_gather(token_block, 'vocab', axis=1, tiled=True)]
  transfers between devices with their start and end apart: 2 -> 9, of which waited for: 2 -> 9; matrix products, arithmetic and copies ran while one was open for 2% -> 2% of each run, Pallas kernels for 0% -> 0%
where the time goes in v1:
time: 227 us; the launch traced here: 226 us
  waiting for transfers between devices  155 us (68%)
  matrix products  37.8 us (17%)
  between operations  16 us (7%)
  starting transfers between devices  14.3 us (6%)
  other arithmetic  2.78 us (1%)
    all_gather x1, waiting for transfers between devices, shards(): features = lax.all_gather(token_block, 'vocab', axis=1, tiled=True)  90 us
    all_gather x1, waiting for transfers between devices, shards(): token_block = lax.all_gather(hidden, 'grp', axis=0, tiled=True)  51.4 us
    dot_general x1, matrix products, shards(): lax.dot_general(grads, features, (((0,), (0,)), ((), ())), preferred_elem...  19.5 us
    dot_general x1, matrix products, shards(): lax.dot_general(features, head_weight, (((1,), (1,)), ((), ())), preferre...  16.3 us
    ppermute x7, starting transfers between devices, butterfly(): stats = combine(stats, lax.ppermute(stats, axis, perm))  14.2 us
    ppermute x7, waiting for transfers between devices, butterfly(): stats = combine(stats, lax.ppermute(stats, axis, perm))  12.7 us
  transfers between devices with their start and end apart: 9, of which 9 were waited for; matrix products, arithmetic and copies ran while one was open for 2% of the time, Pallas kernels for 0%

profile of v1, /device:TPU:0, one launch (start us, length us, event | category | flops | bytes accessed | tf_op | source)
XLA Modules:
  0.0 226.4 jit_solution(9675438265571959442)
XLA Ops:
  7.2 0.0 all-gather.3.cloned.1.call-start
  7.2 0.7 all-gather.3.cloned.1.call-update
  7.9 0.0 all-gather.5.cloned.1.call-start
  7.9 51.4 %all-gather.3.cloned.1.call-done = bf16[1024,512]{1,0:T(8,128)(2,1)} async-done(((bf16[128,512]{1,0:T(8,128)(2,1)}), bf16[1024,512]{1,0:T(8,128)(2,1)}) %all-gather.3.cloned.1.call-update) | async-done | bytes 1048592 | tf_op jit(solution)/shard_map/all_gather | solution.py:61
  59.3 0.0 all-gather.5.cloned.1.call-update
  59.3 0.7 convert_element_type.17
  60.0 0.8 copy.13
  60.8 0.2 reduce-window.8
  60.9 0.1 reduce
  61.1 0.2 convert_reduce_fusion
  61.3 0.0 copy-start.3
  61.3 90.0 %all-gather.5.cloned.1.call-done = bf16[1024,8192]{1,0:T(8,128)(2,1)} async-done(((bf16[1024,512]{1,0:T(8,128)(2,1)}), bf16[1024,8192]{1,0:T(8,128)(2,1)}) %all-gather.5.cloned.1.call-update) | async-done | bytes 16777232 | tf_op jit(solution)/shard_map/all_gather | solution.py:62
  151.3 16.3 %fusion.53 = (f32[1024]{0:T(1024)S(1)}, f32[1024,640]{0,1:T(8,128)S(1)}) fusion(bf16[1024,8192]{1,0:T(8,128)(2,1)} %all-gather.5.cloned.1.call-done, bf16[640,8192]{1,0:T(8,128)(2,1)} %param.9), kind=kOutput, calls=%fused_computation.105 | convolution fusion | flops 10738072576 | bytes 29888512 | tf_op jit(solution)/shard_map/dot_general | solution.py:66
  167.6 0.0 copy-start.4
  167.6 0.0 copy-start.5
  167.6 0.0 copy-start
  167.6 0.0 copy-start.1
  167.6 0.0 copy-done.3
  167.6 0.6 exponential_reduce_fusion
  168.3 0.3 collective-permute-start
  168.6 0.4 fusion.19
  169.0 0.6 collective-permute-done
  169.6 1.4 collective-permute-start.1
  171.0 0.4 fusion.21
  171.4 2.0 collective-permute-done.1
  173.5 1.6 collective-permute-start.2
  175.1 0.0 copy-done.4
  175.1 0.0 copy-done.5
  175.1 0.2 fusion.15
  175.3 2.1 collective-permute-done.2
  177.4 2.8 %collective-permute-start.3 = (f32[3,1024]{1,0:T(4,128)S(1)}, f32[3,1024]{1,0:T(4,128)S(1)}, u32[]{:S(2)}, u32[]{:S(2)}) collective-permute-start(f32[3,1024]{1,0:T(4,128)S(1)} %pad_maximum_fusion.3), channel_id=1, source_target_pairs={{0,8},{1,9},{2,10},{3,11},{4,12},{5,13},{6,14},{7,15},{8,0},{9,1},... | collective-permute-start | bytes 36872 | tf_op jit(solution)/shard_map/ppermute | solution.py:53
  180.2 0.2 fusion.13
  180.4 2.3 %collective-permute-done.3 = f32[3,1024]{1,0:T(4,128)S(1)} collective-permute-done((f32[3,1024]{1,0:T(4,128)S(1)}, f32[3,1024]{1,0:T(4,128)S(1)}, u32[]{:S(2)}, u32[]{:S(2)}) %collective-permute-start.3) | collective-permute-done | bytes 12320 | tf_op jit(solution)/shard_map/ppermute | solution.py:53
  182.8 1.6 collective-permute-start.4
  184.4 0.2 fusion.12
  184.6 2.0 collective-permute-done.4
  186.6 3.2 %collective-permute-start.5 = (f32[3,1024]{1,0:T(4,128)S(1)}, f32[3,1024]{1,0:T(4,128)S(1)}, u32[]{:S(2)}, u32[]{:S(2)}) collective-permute-start(f32[3,1024]{1,0:T(4,128)S(1)} %pad_maximum_fusion.5), channel_id=1, source_target_pairs={{0,32},{16,48},{32,0},{48,16},{64,96},{80,112},{96,64},{112,80},{1... | collective-permute-start | bytes 36872 | tf_op jit(solution)/shard_map/ppermute | solution.py:53
  189.9 0.2 fusion.17
  190.1 1.9 collective-permute-done.5
  192.0 3.2 %collective-permute-start.6 = (f32[3,1024]{1,0:T(4,128)S(1)}, f32[3,1024]{1,0:T(4,128)S(1)}, u32[]{:S(2)}, u32[]{:S(2)}) collective-permute-start(f32[3,1024]{1,0:T(4,128)S(1)} %pad_maximum_fusion.6), channel_id=1, source_target_pairs={{0,64},{16,80},{32,96},{48,112},{64,0},{80,16},{96,32},{112,48},{1... | collective-permute-start | bytes 36872 | tf_op jit(solution)/shard_map/ppermute | solution.py:53
  195.2 0.4 fusion.20
  195.7 1.8 collective-permute-done.6
  197.5 0.0 copy-done
  197.5 0.0 copy-done.1
  197.5 0.1 fusion.29
  197.6 0.0 copy-start.2
  197.6 0.6 multiply_reduce_fusion
  198.9 19.5 %convolution_convert_fusion = bf16[640,8192]{1,0:T(8,128)(2,1)} fusion(bf16[1024,8192]{1,0:T(8,128)(2,1)} %all-gather.5.cloned.1.call-done, f32[1024,640]{0,1:T(8,128)S(1)} %get-tuple-element.58, f32[1024]{0:T(1024)S(1)} %get-tuple-element.7, f32[1024]{0:T(1024)S(1)} %get-tuple-element.5, s32[1024]{0:T(1024)S(1)} %copy-done.3, s32[640]{0:T(1024)S(1)} %iota_add_fusion), kind=kOutput, calls=%fused_computation | convolution fusion | flops 10746593280 | bytes 29899264 | tf_op jit(solution)/shard_map/dot_general | solution.py:82
  218.4 0.0 copy-done.2
  (15 shorter events, 0.3 us)
Async XLA Ops:
  7.2 52.1 %all-gather.3.cloned.1.call-start = ((), (), s32[]{:S(2)}) async-start(), calls=%async_computation | async-start | bytes 1179648 | tf_op jit(solution)/shard_map/all_gather | solution.py:61
  7.9 143.4 %all-gather.5.cloned.1.call-start = ((), (), s32[]{:S(2)}) async-start(), calls=%async_computation.1 | async-start | bytes 17825792 | tf_op jit(solution)/shard_map/all_gather | solution.py:62
  61.3 106.3 %copy-start.3 = (s32[1024]{0:T(1024)S(1)}, s32[1024]{0:T(1024)}, u32[]{:S(2)}) copy-start(s32[1024]{0:T(1024)} %param.10) | copy-start | bytes 12292
  167.6 7.5 %copy-start.4 = (f32[128]{0:T(128)S(1)}, f32[128]{0:T(128)}, u32[]{:S(2)}) copy-start(f32[128]{0:T(128)} %param.15) | copy-start | bytes 1540
  167.6 7.5 %copy-start.5 = (s32[128]{0:T(128)S(1)}, s32[128]{0:T(128)}, u32[]{:S(2)}) copy-start(s32[128]{0:T(128)} %param.14) | copy-start | bytes 1540
  167.6 29.9 %copy-start = (s32[1024]{0:T(1024)S(1)}, s32[1024]{0:T(1024)}, u32[]{:S(2)}) copy-start(s32[1024]{0:T(1024)} %param.12) | copy-start | bytes 12292
  167.6 29.9 %copy-start.1 = (f32[1024]{0:T(1024)S(1)}, f32[1024]{0:T(1024)}, u32[]{:S(2)}) copy-start(f32[1024]{0:T(1024)} %param.11) | copy-start | bytes 12292
  168.3 1.3 collective-permute-start
  169.6 3.8 %collective-permute-start.1 = (f32[3,1024]{1,0:T(4,128)S(1)}, f32[3,1024]{1,0:T(4,128)S(1)}, u32[]{:S(2)}, u32[]{:S(2)}) collective-permute-start(f32[3,1024]{1,0:T(4,128)S(1)} %pad_maximum_fusion.1), channel_id=1, source_target_pairs={{0,2},{1,3},{2,0},{3,1},{4,6},{5,7},{6,4},{7,5},{8,10},{9,11},{10,... | collective-permute-start | bytes 36872 | tf_op jit(solution)/shard_map/ppermute | solution.py:53
  173.5 3.8 %collective-permute-start.2 = (f32[3,1024]{1,0:T(4,128)S(1)}, f32[3,1024]{1,0:T(4,128)S(1)}, u32[]{:S(2)}, u32[]{:S(2)}) collective-permute-start(f32[3,1024]{1,0:T(4,128)S(1)} %pad_maximum_fusion.2), channel_id=1, source_target_pairs={{0,4},{1,5},{2,6},{3,7},{4,0},{5,1},{6,2},{7,3},{8,12},{9,13},{10,... | collective-permute-start | bytes 36872 | tf_op jit(solution)/shard_map/ppermute | solution.py:53
  177.4 5.3 %collective-permute-start.3 = (f32[3,1024]{1,0:T(4,128)S(1)}, f32[3,1024]{1,0:T(4,128)S(1)}, u32[]{:S(2)}, u32[]{:S(2)}) collective-permute-start(f32[3,1024]{1,0:T(4,128)S(1)} %pad_maximum_fusion.3), channel_id=1, source_target_pairs={{0,8},{1,9},{2,10},{3,11},{4,12},{5,13},{6,14},{7,15},{8,0},{9,1},... | collective-permute-start | bytes 36872 | tf_op jit(solution)/shard_map/ppermute | solution.py:53
  182.8 3.8 %collective-permute-start.4 = (f32[3,1024]{1,0:T(4,128)S(1)}, f32[3,1024]{1,0:T(4,128)S(1)}, u32[]{:S(2)}, u32[]{:S(2)}) collective-permute-start(f32[3,1024]{1,0:T(4,128)S(1)} %pad_maximum_fusion.4), channel_id=1, source_target_pairs={{0,16},{16,0},{32,48},{48,32},{64,80},{80,64},{96,112},{112,96},{1... | collective-permute-start | bytes 36872 | tf_op jit(solution)/shard_map/ppermute | solution.py:53
  186.6 5.3 %collective-permute-start.5 = (f32[3,1024]{1,0:T(4,128)S(1)}, f32[3,1024]{1,0:T(4,128)S(1)}, u32[]{:S(2)}, u32[]{:S(2)}) collective-permute-start(f32[3,1024]{1,0:T(4,128)S(1)} %pad_maximum_fusion.5), channel_id=1, source_target_pairs={{0,32},{16,48},{32,0},{48,16},{64,96},{80,112},{96,64},{112,80},{1... | collective-permute-start | bytes 36872 | tf_op jit(solution)/shard_map/ppermute | solution.py:53
  192.0 5.5 %collective-permute-start.6 = (f32[3,1024]{1,0:T(4,128)S(1)}, f32[3,1024]{1,0:T(4,128)S(1)}, u32[]{:S(2)}, u32[]{:S(2)}) collective-permute-start(f32[3,1024]{1,0:T(4,128)S(1)} %pad_maximum_fusion.6), channel_id=1, source_target_pairs={{0,64},{16,80},{32,96},{48,112},{64,0},{80,16},{96,32},{112,48},{1... | collective-permute-start | bytes 36872 | tf_op jit(solution)/shard_map/ppermute | solution.py:53
  197.6 20.8 %copy-start.2 = (f32[1024]{0:T(1024)}, f32[1024]{0:T(1024)S(1)}, u32[]{:S(2)}) copy-start(f32[1024]{0:T(1024)S(1)} %get-tuple-element.6) | copy-start | bytes 12292
Sparse Core Ops, SparseCore 0:
  10.3 48.9 all-gather.2
  61.0 90.2 all-gather.4

commit v2 on v1

--- a/solution.py
+++ b/solution.py
@@ -55,10 +55,27 @@
     return stats[0], stats[1], stats[2]
 
 
+def doubling_gather(block, axis):
+    size = lax.axis_size(axis)
+    index = lax.axis_index(axis)
+    step = 1
+    while step < size:
+        perm = [(i, i ^ step) for i in range(size)]
+        theirs = lax.ppermute(block, axis, perm)
+        upper = (index & step) != 0
+        block = jnp.where(
+            upper,
+            jnp.concatenate([theirs, block], axis=0),
+            jnp.concatenate([block, theirs], axis=0),
+        )
+        step *= 2
+    return block
+
+
 def shards(
     hidden, head_weight, targets, old_logprobs, loss_mask, beam_lengths, beam_group, rewards
 ):
-    token_block = lax.all_gather(hidden, "grp", axis=0, tiled=True)
+    token_block = doubling_gather(hidden, "grp")
     features = lax.all_gather(token_block, "vocab", axis=1, tiled=True)
     shard = head_weight.shape[0]
     offset = (lax.axis_index("grp") * lax.axis_size("vocab") + lax.axis_index("vocab")) * shard

time: 227 us -> 207 us (0.912)
  waiting for transfers between devices: 155 us -> 125 us
  starting transfers between devices: 14.3 us -> 23.2 us
    all_gather x1 -> x0, waiting for transfers between devices: 51.4 us -> none  [shards(): token_block = lax.all_gather(hidden, 'grp', axis=0, tiled=True)]
    ppermute x0 -> x3, waiting for transfers between devices: none -> 19.9 us  [doubling_gather(): theirs = lax.ppermute(block, axis, perm)]
    ppermute x0 -> x3, starting transfers between devices: none -> 8.99 us  [doubling_gather(): theirs = lax.ppermute(block, axis, perm)]
    select_n x0 -> x3, other arithmetic: none -> 2.68 us  [doubling_gather(): jnp.where(upper, jnp.concatenate([theirs, block], axis=0), jnp.concatenat...]
    all_gather x1, waiting for transfers between devices: 90 us -> 92.5 us  [shards(): features = lax.all_gather(token_block, 'vocab', axis=1, tiled=True)]
  transfers between devices with their start and end apart: 9 -> 11, of which waited for: 9 -> 11; matrix products, arithmetic and copies ran while one was open for 2% -> 1% of each run, Pallas kernels for 0% -> 0%
where the time goes in v2:
time: 207 us
  waiting for transfers between devices  125 us (60%)
  matrix products  37.8 us (18%)
  starting transfers between devices  23.2 us (11%)
  between operations  16 us (8%)
  other arithmetic  4.78 us (2%)
    all_gather x1, waiting for transfers between devices, shards(): features = lax.all_gather(token_block, 'vocab', axis=1, tiled=True)  92.5 us
    ppermute x3, waiting for transfers between devices, doubling_gather(): theirs = lax.ppermute(block, axis, perm)  19.9 us
    dot_general x1, matrix products, shards(): lax.dot_general(grads, features, (((0,), (0,)), ((), ())), preferred_elem...  19.5 us
    dot_general x1, matrix products, shards(): lax.dot_general(features, head_weight, (((1,), (1,)), ((), ())), preferre...  16.3 us
    ppermute x7, starting transfers between devices, butterfly(): stats = combine(stats, lax.ppermute(stats, axis, perm))  14.2 us
    ppermute x7, waiting for transfers between devices, butterfly(): stats = combine(stats, lax.ppermute(stats, axis, perm))  12.7 us
    ppermute x3, starting transfers between devices, doubling_gather(): theirs = lax.ppermute(block, axis, perm)  8.99 us
  transfers between devices with their start and end apart: 11, of which 11 were waited for; matrix products, arithmetic and copies ran while one was open for 1% of the time, Pallas kernels for 0%

profile of v2, /device:TPU:0, one launch (start us, length us, event | category | flops | bytes accessed | tf_op | source)
XLA Modules:
  0.0 207.0 jit_solution(2376802297908729681)
XLA Ops:
  7.2 0.0 copy-start
  7.2 0.0 copy-start.4
  7.2 0.0 all-gather.2.cloned.1.call-start
  7.2 2.1 %collective-permute-start = (bf16[128,512]{1,0:T(8,128)(2,1)}, bf16[128,512]{1,0:T(8,128)(2,1)S(1)}, u32[]{:S(2)}, u32[]{:S(2)}) collective-permute-start(bf16[128,512]{1,0:T(8,128)(2,1)} %param.8), channel_id=1, source_target_pairs={{0,16},{16,0},{32,48},{48,32},{64,80},{80,64},{96,112},{112,96},{1... | collective-permute-start | bytes 393224 | tf_op jit(solution)/shard_map/ppermute | solution.py:64
  9.3 3.7 %collective-permute-done = bf16[128,512]{1,0:T(8,128)(2,1)S(1)} collective-permute-done((bf16[128,512]{1,0:T(8,128)(2,1)}, bf16[128,512]{1,0:T(8,128)(2,1)S(1)}, u32[]{:S(2)}, u32[]{:S(2)}) %collective-permute-start) | collective-permute-done | bytes 131104 | tf_op jit(solution)/shard_map/ppermute | solution.py:64
  13.0 1.0 maximum_select_fusion.2
  14.1 3.8 %collective-permute-start.1 = (bf16[256,512]{1,0:T(8,128)(2,1)S(1)}, bf16[256,512]{1,0:T(8,128)(2,1)S(1)}, u32[]{:S(2)}, u32[]{:S(2)}) collective-permute-start(bf16[256,512]{1,0:T(8,128)(2,1)S(1)} %maximum_select_fusion.2), channel_id=1, source_target_pairs={{0,32},{16,48},{32,0},{48,16},{64,96},{80,112},{96,64},{112,80},{1... | collective-permute-start | bytes 786440 | tf_op jit(solution)/shard_map/ppermute | solution.py:64
  17.9 5.5 %collective-permute-done.1 = bf16[256,512]{1,0:T(8,128)(2,1)S(1)} collective-permute-done((bf16[256,512]{1,0:T(8,128)(2,1)S(1)}, bf16[256,512]{1,0:T(8,128)(2,1)S(1)}, u32[]{:S(2)}, u32[]{:S(2)}) %collective-permute-start.1) | collective-permute-done | bytes 262176 | tf_op jit(solution)/shard_map/ppermute | solution.py:64
  23.3 0.2 maximum_select_fusion.1
  23.5 3.1 %collective-permute-start.2 = (bf16[512,512]{1,0:T(8,128)(2,1)S(1)}, bf16[512,512]{1,0:T(8,128)(2,1)S(1)}, u32[]{:S(2)}, u32[]{:S(2)}) collective-permute-start(bf16[512,512]{1,0:T(8,128)(2,1)S(1)} %maximum_select_fusion.1), channel_id=1, source_target_pairs={{0,64},{16,80},{32,96},{48,112},{64,0},{80,16},{96,32},{112,48},{1... | collective-permute-start | bytes 1572872 | tf_op jit(solution)/shard_map/ppermute | solution.py:64
  26.6 10.7 %collective-permute-done.2 = bf16[512,512]{1,0:T(8,128)(2,1)S(1)} collective-permute-done((bf16[512,512]{1,0:T(8,128)(2,1)S(1)}, bf16[512,512]{1,0:T(8,128)(2,1)S(1)}, u32[]{:S(2)}, u32[]{:S(2)}) %collective-permute-start.2) | collective-permute-done | bytes 524320 | tf_op jit(solution)/shard_map/ppermute | solution.py:64
  37.4 1.4 maximum_select_fusion
  38.8 0.0 all-gather.2.cloned.1.call-update
  38.8 0.0 copy-done
  38.8 0.0 copy-done.4
  38.8 0.1 copy.13
  39.0 0.2 reduce-window.8
  39.1 0.1 reduce
  39.2 0.2 convert_reduce_fusion
  39.5 0.0 copy-start.3
  39.5 92.5 %all-gather.2.cloned.1.call-done = bf16[1024,8192]{1,0:T(8,128)(2,1)} async-done(((bf16[1024,512]{1,0:T(8,128)(2,1)}), bf16[1024,8192]{1,0:T(8,128)(2,1)}) %all-gather.2.cloned.1.call-update) | async-done | bytes 16777232 | tf_op jit(solution)/shard_map/all_gather | solution.py:79
  132.0 16.3 %fusion.53 = (f32[1024]{0:T(1024)S(1)}, f32[1024,640]{0,1:T(8,128)S(1)}) fusion(bf16[1024,8192]{1,0:T(8,128)(2,1)} %all-gather.2.cloned.1.call-done, bf16[640,8192]{1,0:T(8,128)(2,1)} %param.9), kind=kOutput, calls=%fused_computation.108 | convolution fusion | flops 10738072576 | bytes 29888512 | tf_op jit(solution)/shard_map/dot_general | solution.py:83
  148.3 0.0 copy-start.5
  148.3 0.0 copy-start.6
  148.3 0.0 copy-start.1
  148.3 0.0 copy-done.3
  148.3 0.6 exponential_reduce_fusion
  149.0 0.3 collective-permute-start.3
  149.3 0.4 fusion.19
  149.7 0.6 collective-permute-done.3
  150.3 1.4 collective-permute-start.4
  151.7 0.4 fusion.21
  152.1 2.0 collective-permute-done.4
  154.2 1.6 collective-permute-start.5
  155.7 0.0 copy-done.5
  155.7 0.0 copy-done.6
  155.7 0.2 fusion.15
  155.9 2.1 collective-permute-done.5
  158.0 2.8 %collective-permute-start.6 = (f32[3,1024]{1,0:T(4,128)S(1)}, f32[3,1024]{1,0:T(4,128)S(1)}, u32[]{:S(2)}, u32[]{:S(2)}) collective-permute-start(f32[3,1024]{1,0:T(4,128)S(1)} %pad_maximum_fusion.3), channel_id=1, source_target_pairs={{0,8},{1,9},{2,10},{3,11},{4,12},{5,13},{6,14},{7,15},{8,0},{9,1},... | collective-permute-start | bytes 36872 | tf_op jit(solution)/shard_map/ppermute | solution.py:53
  160.8 0.2 fusion.13
  161.0 2.3 %collective-permute-done.6 = f32[3,1024]{1,0:T(4,128)S(1)} collective-permute-done((f32[3,1024]{1,0:T(4,128)S(1)}, f32[3,1024]{1,0:T(4,128)S(1)}, u32[]{:S(2)}, u32[]{:S(2)}) %collective-permute-start.6) | collective-permute-done | bytes 12320 | tf_op jit(solution)/shard_map/ppermute | solution.py:53
  163.4 1.6 collective-permute-start.7
  165.1 0.2 fusion.12
  165.2 2.0 collective-permute-done.7
  167.3 3.2 %collective-permute-start.8 = (f32[3,1024]{1,0:T(4,128)S(1)}, f32[3,1024]{1,0:T(4,128)S(1)}, u32[]{:S(2)}, u32[]{:S(2)}) collective-permute-start(f32[3,1024]{1,0:T(4,128)S(1)} %pad_maximum_fusion.5), channel_id=1, source_target_pairs={{0,32},{16,48},{32,0},{48,16},{64,96},{80,112},{96,64},{112,80},{1... | collective-permute-start | bytes 36872 | tf_op jit(solution)/shard_map/ppermute | solution.py:53
  170.5 0.2 fusion.17
  170.7 1.9 collective-permute-done.8
  172.7 3.2 %collective-permute-start.9 = (f32[3,1024]{1,0:T(4,128)S(1)}, f32[3,1024]{1,0:T(4,128)S(1)}, u32[]{:S(2)}, u32[]{:S(2)}) collective-permute-start(f32[3,1024]{1,0:T(4,128)S(1)} %pad_maximum_fusion.6), channel_id=1, source_target_pairs={{0,64},{16,80},{32,96},{48,112},{64,0},{80,16},{96,32},{112,48},{1... | collective-permute-start | bytes 36872 | tf_op jit(solution)/shard_map/ppermute | solution.py:53
  175.9 0.4 fusion.20
  176.4 1.8 collective-permute-done.9
  178.2 0.0 copy-done.1
  178.2 0.1 fusion.29
  178.3 0.0 copy-start.2
  178.3 0.6 multiply_reduce_fusion
  179.5 19.5 %convolution_convert_fusion = bf16[640,8192]{1,0:T(8,128)(2,1)} fusion(bf16[1024,8192]{1,0:T(8,128)(2,1)} %all-gather.2.cloned.1.call-done, f32[1024,640]{0,1:T(8,128)S(1)} %get-tuple-element.58, f32[1024]{0:T(1024)S(1)} %get-tuple-element.7, f32[1024]{0:T(1024)S(1)} %get-tuple-element.5, s32[1024]{0:T(1024)S(1)} %copy-done.3, s32[640]{0:T(1024)S(1)} %iota_add_fusion), kind=kOutput, calls=%fused_computation | convolution fusion | flops 10746593280 | bytes 29899264 | tf_op jit(solution)/shard_map/dot_general | solution.py:99
  199.0 0.0 copy-done.2
  (16 shorter events, 0.3 us)
Async XLA Ops:
  7.2 31.6 %copy-start = (s32[1024]{0:T(1024)S(1)}, s32[1024]{0:T(1024)}, u32[]{:S(2)}) copy-start(s32[1024]{0:T(1024)} %param.12) | copy-start | bytes 12292
  7.2 31.7 %copy-start.4 = (s32[128]{0:T(128)S(1)}, s32[128]{0:T(128)}, u32[]{:S(2)}) copy-start(s32[128]{0:T(128)} %param.13) | copy-start | bytes 1540
  7.2 124.8 %all-gather.2.cloned.1.call-start = ((), (), s32[]{:S(2)}) async-start(), calls=%async_computation | async-start | bytes 17825792 | tf_op jit(solution)/shard_map/all_gather | solution.py:79
  7.2 5.8 %collective-permute-start = (bf16[128,512]{1,0:T(8,128)(2,1)}, bf16[128,512]{1,0:T(8,128)(2,1)S(1)}, u32[]{:S(2)}, u32[]{:S(2)}) collective-permute-start(bf16[128,512]{1,0:T(8,128)(2,1)} %param.8), channel_id=1, source_target_pairs={{0,16},{16,0},{32,48},{48,32},{64,80},{80,64},{96,112},{112,96},{1... | collective-permute-start | bytes 393224 | tf_op jit(solution)/shard_map/ppermute | solution.py:64
  14.1 9.2 %collective-permute-start.1 = (bf16[256,512]{1,0:T(8,128)(2,1)S(1)}, bf16[256,512]{1,0:T(8,128)(2,1)S(1)}, u32[]{:S(2)}, u32[]{:S(2)}) collective-permute-start(bf16[256,512]{1,0:T(8,128)(2,1)S(1)} %maximum_select_fusion.2), channel_id=1, source_target_pairs={{0,32},{16,48},{32,0},{48,16},{64,96},{80,112},{96,64},{112,80},{1... | collective-permute-start | bytes 786440 | tf_op jit(solution)/shard_map/ppermute | solution.py:64
  23.5 13.8 %collective-permute-start.2 = (bf16[512,512]{1,0:T(8,128)(2,1)S(1)}, bf16[512,512]{1,0:T(8,128)(2,1)S(1)}, u32[]{:S(2)}, u32[]{:S(2)}) collective-permute-start(bf16[512,512]{1,0:T(8,128)(2,1)S(1)} %maximum_select_fusion.1), channel_id=1, source_target_pairs={{0,64},{16,80},{32,96},{48,112},{64,0},{80,16},{96,32},{112,48},{1... | collective-permute-start | bytes 1572872 | tf_op jit(solution)/shard_map/ppermute | solution.py:64
  39.5 108.8 %copy-start.3 = (s32[1024]{0:T(1024)S(1)}, s32[1024]{0:T(1024)}, u32[]{:S(2)}) copy-start(s32[1024]{0:T(1024)} %param.10) | copy-start | bytes 12292
  148.3 7.5 %copy-start.5 = (f32[128]{0:T(128)S(1)}, f32[128]{0:T(128)}, u32[]{:S(2)}) copy-start(f32[128]{0:T(128)} %param.15) | copy-start | bytes 1540
  148.3 7.5 %copy-start.6 = (s32[128]{0:T(128)S(1)}, s32[128]{0:T(128)}, u32[]{:S(2)}) copy-start(s32[128]{0:T(128)} %param.14) | copy-start | bytes 1540
  148.3 29.9 %copy-start.1 = (f32[1024]{0:T(1024)S(1)}, f32[1024]{0:T(1024)}, u32[]{:S(2)}) copy-start(f32[1024]{0:T(1024)} %param.11) | copy-start | bytes 12292
  149.0 1.3 collective-permute-start.3
  150.3 3.8 %collective-permute-start.4 = (f32[3,1024]{1,0:T(4,128)S(1)}, f32[3,1024]{1,0:T(4,128)S(1)}, u32[]{:S(2)}, u32[]{:S(2)}) collective-permute-start(f32[3,1024]{1,0:T(4,128)S(1)} %pad_maximum_fusion.1), channel_id=1, source_target_pairs={{0,2},{1,3},{2,0},{3,1},{4,6},{5,7},{6,4},{7,5},{8,10},{9,11},{10,... | collective-permute-start | bytes 36872 | tf_op jit(solution)/shard_map/ppermute | solution.py:53
  154.2 3.8 %collective-permute-start.5 = (f32[3,1024]{1,0:T(4,128)S(1)}, f32[3,1024]{1,0:T(4,128)S(1)}, u32[]{:S(2)}, u32[]{:S(2)}) collective-permute-start(f32[3,1024]{1,0:T(4,128)S(1)} %pad_maximum_fusion.2), channel_id=1, source_target_pairs={{0,4},{1,5},{2,6},{3,7},{4,0},{5,1},{6,2},{7,3},{8,12},{9,13},{10,... | collective-permute-start | bytes 36872 | tf_op jit(solution)/shard_map/ppermute | solution.py:53
  158.0 5.3 %collective-permute-start.6 = (f32[3,1024]{1,0:T(4,128)S(1)}, f32[3,1024]{1,0:T(4,128)S(1)}, u32[]{:S(2)}, u32[]{:S(2)}) collective-permute-start(f32[3,1024]{1,0:T(4,128)S(1)} %pad_maximum_fusion.3), channel_id=1, source_target_pairs={{0,8},{1,9},{2,10},{3,11},{4,12},{5,13},{6,14},{7,15},{8,0},{9,1},... | collective-permute-start | bytes 36872 | tf_op jit(solution)/shard_map/ppermute | solution.py:53
  163.4 3.8 %collective-permute-start.7 = (f32[3,1024]{1,0:T(4,128)S(1)}, f32[3,1024]{1,0:T(4,128)S(1)}, u32[]{:S(2)}, u32[]{:S(2)}) collective-permute-start(f32[3,1024]{1,0:T(4,128)S(1)} %pad_maximum_fusion.4), channel_id=1, source_target_pairs={{0,16},{16,0},{32,48},{48,32},{64,80},{80,64},{96,112},{112,96},{1... | collective-permute-start | bytes 36872 | tf_op jit(solution)/shard_map/ppermute | solution.py:53
  167.3 5.3 %collective-permute-start.8 = (f32[3,1024]{1,0:T(4,128)S(1)}, f32[3,1024]{1,0:T(4,128)S(1)}, u32[]{:S(2)}, u32[]{:S(2)}) collective-permute-start(f32[3,1024]{1,0:T(4,128)S(1)} %pad_maximum_fusion.5), channel_id=1, source_target_pairs={{0,32},{16,48},{32,0},{48,16},{64,96},{80,112},{96,64},{112,80},{1... | collective-permute-start | bytes 36872 | tf_op jit(solution)/shard_map/ppermute | solution.py:53
  172.7 5.5 %collective-permute-start.9 = (f32[3,1024]{1,0:T(4,128)S(1)}, f32[3,1024]{1,0:T(4,128)S(1)}, u32[]{:S(2)}, u32[]{:S(2)}) collective-permute-start(f32[3,1024]{1,0:T(4,128)S(1)} %pad_maximum_fusion.6), channel_id=1, source_target_pairs={{0,64},{16,80},{32,96},{48,112},{64,0},{80,16},{96,32},{112,48},{1... | collective-permute-start | bytes 36872 | tf_op jit(solution)/shard_map/ppermute | solution.py:53
  178.3 20.8 %copy-start.2 = (f32[1024]{0:T(1024)}, f32[1024]{0:T(1024)S(1)}, u32[]{:S(2)}) copy-start(f32[1024]{0:T(1024)S(1)} %get-tuple-element.6) | copy-start | bytes 12292
Sparse Core Ops, SparseCore 0:
  38.9 92.9 all-gather.1

commit v3 on v1

--- a/solution.py
+++ b/solution.py
@@ -55,10 +55,19 @@
     return stats[0], stats[1], stats[2]
 
 
+def peer_gather(block, axis):
+    size = lax.axis_size(axis)
+    index = lax.axis_index(axis)
+    got = [block] + [lax.ppermute(block, axis, [(i, i ^ k) for i in range(size)]) for k in range(1, size)]
+    order = index ^ jnp.arange(size, dtype=jnp.int32)
+    stacked = jnp.take(jnp.stack(got), order, axis=0)
+    return stacked.reshape(size * block.shape[0], *block.shape[1:])
+
+
 def shards(
     hidden, head_weight, targets, old_logprobs, loss_mask, beam_lengths, beam_group, rewards
 ):
-    token_block = lax.all_gather(hidden, "grp", axis=0, tiled=True)
+    token_block = peer_gather(hidden, "grp")
     features = lax.all_gather(token_block, "vocab", axis=1, tiled=True)
     shard = head_weight.shape[0]
     offset = (lax.axis_index("grp") * lax.axis_size("vocab") + lax.axis_index("vocab")) * shard

time: 227 us -> 204 us (0.90)
  waiting for transfers between devices: 155 us -> 115 us
  starting transfers between devices: 14.3 us -> 29.7 us
    all_gather x1 -> x0, waiting for transfers between devices: 51.4 us -> none  [shards(): token_block = lax.all_gather(hidden, 'grp', axis=0, tiled=True)]
    ppermute x0 -> x7, starting transfers between devices: none -> 15.4 us  [peer_gather(): lax.ppermute(block, axis, [(i, i ^ k) for i in range(size)])]
    ppermute x0 -> x7, waiting for transfers between devices: none -> 13 us  [peer_gather(): lax.ppermute(block, axis, [(i, i ^ k) for i in range(size)])]
  transfers between devices with their start and end apart: 9 -> 15, of which waited for: 9 -> 10; matrix products, arithmetic and copies ran while one was open for 2% -> 2% of each run, Pallas kernels for 0% -> 0%
where the time goes in v3:
time: 204 us
  waiting for transfers between devices  115 us (56%)
  matrix products  37.9 us (19%)
  starting transfers between devices  29.7 us (15%)
  between operations  16.1 us (8%)
  other arithmetic  3.3 us (2%)
    all_gather x1, waiting for transfers between devices, shards(): features = lax.all_gather(token_block, 'vocab', axis=1, tiled=True)  89 us
    dot_general x1, matrix products, shards(): lax.dot_general(grads, features, (((0,), (0,)), ((), ())), preferred_elem...  19.6 us
    dot_general x1, matrix products, shards(): lax.dot_general(features, head_weight, (((1,), (1,)), ((), ())), preferre...  16.3 us
    ppermute x7, starting transfers between devices, peer_gather(): lax.ppermute(block, axis, [(i, i ^ k) for i in range(size)])  15.4 us
    ppermute x7, starting transfers between devices, butterfly(): stats = combine(stats, lax.ppermute(stats, axis, perm))  14.2 us
    ppermute x7, waiting for transfers between devices, peer_gather(): lax.ppermute(block, axis, [(i, i ^ k) for i in range(size)])  13 us
    ppermute x7, waiting for transfers between devices, butterfly(): stats = combine(stats, lax.ppermute(stats, axis, perm))  12.7 us
  transfers between devices with their start and end apart: 15, of which 10 were waited for; matrix products, arithmetic and copies ran while one was open for 2% of the time, Pallas kernels for 0%

profile of v3, /device:TPU:0, one launch (start us, length us, event | category | flops | bytes accessed | tf_op | source)
XLA Modules:
  0.0 203.6 jit_solution(3739752639197690326)
XLA Ops:
  7.2 0.0 all-gather.2.cloned.1.call-start
  7.2 4.6 %collective-permute-start.4 = (bf16[128,512]{1,0:T(8,128)(2,1)}, bf16[128,512]{1,0:T(8,128)(2,1)S(1)}, u32[]{:S(2)}, u32[]{:S(2)}) collective-permute-start(bf16[128,512]{1,0:T(8,128)(2,1)} %param.8), channel_id=1, source_target_pairs={{0,80},{16,64},{32,112},{48,96},{64,16},{80,0},{96,48},{112,32},{1... | collective-permute-start | bytes 393224 | tf_op jit(solution)/shard_map/ppermute | solution.py:61
  11.8 0.5 collective-permute-start.3
  12.3 2.5 %collective-permute-start.2 = (bf16[128,512]{1,0:T(8,128)(2,1)}, bf16[128,512]{1,0:T(8,128)(2,1)S(1)}, u32[]{:S(2)}, u32[]{:S(2)}) collective-permute-start(bf16[128,512]{1,0:T(8,128)(2,1)} %param.8), channel_id=1, source_target_pairs={{0,48},{16,32},{32,16},{48,0},{64,112},{80,96},{96,80},{112,64},{1... | collective-permute-start | bytes 393224 | tf_op jit(solution)/shard_map/ppermute | solution.py:61
  14.8 1.1 collective-permute-start.1
  15.9 0.5 collective-permute-start
  16.4 0.9 bitcast_dynamic-update-slice_fusion.7
  17.3 0.1 broadcast_bitcast_fusion
  17.4 4.4 %collective-permute-done = bf16[128,512]{1,0:T(8,128)(2,1)S(1)} collective-permute-done((bf16[128,512]{1,0:T(8,128)(2,1)}, bf16[128,512]{1,0:T(8,128)(2,1)S(1)}, u32[]{:S(2)}, u32[]{:S(2)}) %collective-permute-start) | collective-permute-done | bytes 131104 | tf_op jit(solution)/shard_map/ppermute | solution.py:61
  21.9 5.7 %collective-permute-start.6 = (bf16[128,512]{1,0:T(8,128)(2,1)}, bf16[128,512]{1,0:T(8,128)(2,1)S(1)}, u32[]{:S(2)}, u32[]{:S(2)}) collective-permute-start(bf16[128,512]{1,0:T(8,128)(2,1)} %param.8), channel_id=1, source_target_pairs={{0,112},{16,96},{32,80},{48,64},{64,48},{80,32},{96,16},{112,0},{1... | collective-permute-start | bytes 393224 | tf_op jit(solution)/shard_map/ppermute | solution.py:61
  27.6 0.0 collective-permute-done.1
  27.6 0.5 collective-permute-start.5
  28.2 0.0 collective-permute-done.2
  28.2 0.0 collective-permute-done.3
  28.3 0.0 collective-permute-done.4
  28.3 8.5 %collective-permute-done.5 = bf16[128,512]{1,0:T(8,128)(2,1)S(1)} collective-permute-done((bf16[128,512]{1,0:T(8,128)(2,1)}, bf16[128,512]{1,0:T(8,128)(2,1)S(1)}, u32[]{:S(2)}, u32[]{:S(2)}) %collective-permute-start.5) | collective-permute-done | bytes 131104 | tf_op jit(solution)/shard_map/ppermute | solution.py:61
  36.8 0.0 collective-permute-done.6
  36.9 0.0 copy-start
  36.9 0.0 copy-start.4
  36.9 0.6 gather_fusion
  37.5 1.2 bitcast_select_fusion
  38.7 0.0 all-gather.2.cloned.1.call-update
  38.7 0.0 copy-done
  38.7 0.0 copy-done.4
  38.8 0.1 copy.13
  38.9 0.2 reduce-window.8
  39.0 0.1 reduce
  39.2 0.2 convert_reduce_fusion
  39.4 0.0 copy-start.3
  39.4 89.0 %all-gather.2.cloned.1.call-done = bf16[1024,8192]{1,0:T(8,128)(2,1)} async-done(((bf16[1024,512]{1,0:T(8,128)(2,1)}), bf16[1024,8192]{1,0:T(8,128)(2,1)}) %all-gather.2.cloned.1.call-update) | async-done | bytes 16777232 | tf_op jit(solution)/shard_map/all_gather | solution.py:71
  128.4 16.3 %fusion.54 = (f32[1024]{0:T(1024)S(1)}, f32[1024,640]{0,1:T(8,128)S(1)}) fusion(bf16[1024,8192]{1,0:T(8,128)(2,1)} %all-gather.2.cloned.1.call-done, bf16[640,8192]{1,0:T(8,128)(2,1)} %param.9), kind=kOutput, calls=%fused_computation.121 | convolution fusion | flops 10738072576 | bytes 29888512 | tf_op jit(solution)/shard_map/dot_general | solution.py:75
  144.7 0.0 copy-start.5
  144.7 0.0 copy-start.6
  144.8 0.0 copy-start.1
  144.8 0.0 copy-done.3
  144.8 0.6 exponential_reduce_fusion
  145.4 0.3 collective-permute-start.7
  145.8 0.4 fusion.19
  146.1 0.6 collective-permute-done.7
  146.8 1.4 collective-permute-start.8
  148.1 0.4 fusion.21
  148.6 2.0 collective-permute-done.8
  150.6 1.6 collective-permute-start.9
  152.2 0.0 copy-done.5
  152.2 0.0 copy-done.6
  152.2 0.2 fusion.15
  152.4 2.1 %collective-permute-done.9 = f32[3,1024]{1,0:T(4,128)S(1)} collective-permute-done((f32[3,1024]{1,0:T(4,128)S(1)}, f32[3,1024]{1,0:T(4,128)S(1)}, u32[]{:S(2)}, u32[]{:S(2)}) %collective-permute-start.9) | collective-permute-done | bytes 12320 | tf_op jit(solution)/shard_map/ppermute | solution.py:53
  154.5 2.8 %collective-permute-start.10 = (f32[3,1024]{1,0:T(4,128)S(1)}, f32[3,1024]{1,0:T(4,128)S(1)}, u32[]{:S(2)}, u32[]{:S(2)}) collective-permute-start(f32[3,1024]{1,0:T(4,128)S(1)} %pad_maximum_fusion.3), channel_id=1, source_target_pairs={{0,8},{1,9},{2,10},{3,11},{4,12},{5,13},{6,14},{7,15},{8,0},{9,1},... | collective-permute-start | bytes 36872 | tf_op jit(solution)/shard_map/ppermute | solution.py:53
  157.3 0.2 fusion.13
  157.5 2.3 %collective-permute-done.10 = f32[3,1024]{1,0:T(4,128)S(1)} collective-permute-done((f32[3,1024]{1,0:T(4,128)S(1)}, f32[3,1024]{1,0:T(4,128)S(1)}, u32[]{:S(2)}, u32[]{:S(2)}) %collective-permute-start.10) | collective-permute-done | bytes 12320 | tf_op jit(solution)/shard_map/ppermute | solution.py:53
  159.9 1.6 collective-permute-start.11
  161.5 0.2 fusion.12
  161.7 2.0 collective-permute-done.11
  163.8 3.2 %collective-permute-start.12 = (f32[3,1024]{1,0:T(4,128)S(1)}, f32[3,1024]{1,0:T(4,128)S(1)}, u32[]{:S(2)}, u32[]{:S(2)}) collective-permute-start(f32[3,1024]{1,0:T(4,128)S(1)} %pad_maximum_fusion.5), channel_id=1, source_target_pairs={{0,32},{16,48},{32,0},{48,16},{64,96},{80,112},{96,64},{112,80},{1... | collective-permute-start | bytes 36872 | tf_op jit(solution)/shard_map/ppermute | solution.py:53
  167.0 0.2 fusion.17
  167.2 1.9 collective-permute-done.12
  169.1 3.2 %collective-permute-start.13 = (f32[3,1024]{1,0:T(4,128)S(1)}, f32[3,1024]{1,0:T(4,128)S(1)}, u32[]{:S(2)}, u32[]{:S(2)}) collective-permute-start(f32[3,1024]{1,0:T(4,128)S(1)} %pad_maximum_fusion.6), channel_id=1, source_target_pairs={{0,64},{16,80},{32,96},{48,112},{64,0},{80,16},{96,32},{112,48},{1... | collective-permute-start | bytes 36872 | tf_op jit(solution)/shard_map/ppermute | solution.py:53
  172.4 0.4 fusion.20
  172.8 1.8 collective-permute-done.13
  174.7 0.0 copy-done.1
  174.7 0.1 fusion.29
  174.7 0.0 copy-start.2
  174.7 0.6 multiply_reduce_fusion
  176.0 19.6 %convolution_convert_fusion = bf16[640,8192]{1,0:T(8,128)(2,1)} fusion(bf16[1024,8192]{1,0:T(8,128)(2,1)} %all-gather.2.cloned.1.call-done, f32[1024,640]{0,1:T(8,128)S(1)} %get-tuple-element.58, f32[1024]{0:T(1024)S(1)} %get-tuple-element.7, f32[1024]{0:T(1024)S(1)} %get-tuple-element.5, s32[1024]{0:T(1024)S(1)} %copy-done.3, s32[640]{0:T(1024)S(1)} %iota_add_fusion), kind=kOutput, calls=%fused_computation.1 | convolution fusion | flops 10746593280 | bytes 29899264 | tf_op jit(solution)/shard_map/dot_general | solution.py:91
  (27 shorter events, 0.4 us)
Async XLA Ops:
  7.2 121.3 %all-gather.2.cloned.1.call-start = ((), (), s32[]{:S(2)}) async-start(), calls=%async_computation | async-start | bytes 17825792 | tf_op jit(solution)/shard_map/all_gather | solution.py:71
  7.2 21.0 %collective-permute-start.4 = (bf16[128,512]{1,0:T(8,128)(2,1)}, bf16[128,512]{1,0:T(8,128)(2,1)S(1)}, u32[]{:S(2)}, u32[]{:S(2)}) collective-permute-start(bf16[128,512]{1,0:T(8,128)(2,1)} %param.8), channel_id=1, source_target_pairs={{0,80},{16,64},{32,112},{48,96},{64,16},{80,0},{96,48},{112,32},{1... | collective-permute-start | bytes 393224 | tf_op jit(solution)/shard_map/ppermute | solution.py:61
  11.8 16.4 %collective-permute-start.3 = (bf16[128,512]{1,0:T(8,128)(2,1)}, bf16[128,512]{1,0:T(8,128)(2,1)S(1)}, u32[]{:S(2)}, u32[]{:S(2)}) collective-permute-start(bf16[128,512]{1,0:T(8,128)(2,1)} %param.8), channel_id=1, source_target_pairs={{0,64},{16,80},{32,96},{48,112},{64,0},{80,16},{96,32},{112,48},{1... | collective-permute-start | bytes 393224 | tf_op jit(solution)/shard_map/ppermute | solution.py:61
  12.3 15.9 %collective-permute-start.2 = (bf16[128,512]{1,0:T(8,128)(2,1)}, bf16[128,512]{1,0:T(8,128)(2,1)S(1)}, u32[]{:S(2)}, u32[]{:S(2)}) collective-permute-start(bf16[128,512]{1,0:T(8,128)(2,1)} %param.8), channel_id=1, source_target_pairs={{0,48},{16,32},{32,16},{48,0},{64,112},{80,96},{96,80},{112,64},{1... | collective-permute-start | bytes 393224 | tf_op jit(solution)/shard_map/ppermute | solution.py:61
  14.8 12.8 %collective-permute-start.1 = (bf16[128,512]{1,0:T(8,128)(2,1)}, bf16[128,512]{1,0:T(8,128)(2,1)S(1)}, u32[]{:S(2)}, u32[]{:S(2)}) collective-permute-start(bf16[128,512]{1,0:T(8,128)(2,1)} %param.8), channel_id=1, source_target_pairs={{0,32},{16,48},{32,0},{48,16},{64,96},{80,112},{96,64},{112,80},{1... | collective-permute-start | bytes 393224 | tf_op jit(solution)/shard_map/ppermute | solution.py:61
  15.9 6.0 %collective-permute-start = (bf16[128,512]{1,0:T(8,128)(2,1)}, bf16[128,512]{1,0:T(8,128)(2,1)S(1)}, u32[]{:S(2)}, u32[]{:S(2)}) collective-permute-start(bf16[128,512]{1,0:T(8,128)(2,1)} %param.8), channel_id=1, source_target_pairs={{0,16},{16,0},{32,48},{48,32},{64,80},{80,64},{96,112},{112,96},{1... | collective-permute-start | bytes 393224 | tf_op jit(solution)/shard_map/ppermute | solution.py:61
  21.9 14.9 %collective-permute-start.6 = (bf16[128,512]{1,0:T(8,128)(2,1)}, bf16[128,512]{1,0:T(8,128)(2,1)S(1)}, u32[]{:S(2)}, u32[]{:S(2)}) collective-permute-start(bf16[128,512]{1,0:T(8,128)(2,1)} %param.8), channel_id=1, source_target_pairs={{0,112},{16,96},{32,80},{48,64},{64,48},{80,32},{96,16},{112,0},{1... | collective-permute-start | bytes 393224 | tf_op jit(solution)/shard_map/ppermute | solution.py:61
  27.6 9.2 %collective-permute-start.5 = (bf16[128,512]{1,0:T(8,128)(2,1)}, bf16[128,512]{1,0:T(8,128)(2,1)S(1)}, u32[]{:S(2)}, u32[]{:S(2)}) collective-permute-start(bf16[128,512]{1,0:T(8,128)(2,1)} %param.8), channel_id=1, source_target_pairs={{0,96},{16,112},{32,64},{48,80},{64,32},{80,48},{96,0},{112,16},{1... | collective-permute-start | bytes 393224 | tf_op jit(solution)/shard_map/ppermute | solution.py:61
  36.9 1.9 copy-start
  36.9 1.9 copy-start.4
  39.4 105.4 %copy-start.3 = (s32[1024]{0:T(1024)S(1)}, s32[1024]{0:T(1024)}, u32[]{:S(2)}) copy-start(s32[1024]{0:T(1024)} %param.10) | copy-start | bytes 12292
  144.7 7.5 %copy-start.5 = (f32[128]{0:T(128)S(1)}, f32[128]{0:T(128)}, u32[]{:S(2)}) copy-start(f32[128]{0:T(128)} %param.15) | copy-start | bytes 1540
  144.7 7.4 %copy-start.6 = (s32[128]{0:T(128)S(1)}, s32[128]{0:T(128)}, u32[]{:S(2)}) copy-start(s32[128]{0:T(128)} %param.14) | copy-start | bytes 1540
  144.8 29.9 %copy-start.1 = (f32[1024]{0:T(1024)S(1)}, f32[1024]{0:T(1024)}, u32[]{:S(2)}) copy-start(f32[1024]{0:T(1024)} %param.11) | copy-start | bytes 12292
  145.4 1.3 collective-permute-start.7
  146.8 3.8 %collective-permute-start.8 = (f32[3,1024]{1,0:T(4,128)S(1)}, f32[3,1024]{1,0:T(4,128)S(1)}, u32[]{:S(2)}, u32[]{:S(2)}) collective-permute-start(f32[3,1024]{1,0:T(4,128)S(1)} %pad_maximum_fusion.1), channel_id=1, source_target_pairs={{0,2},{1,3},{2,0},{3,1},{4,6},{5,7},{6,4},{7,5},{8,10},{9,11},{10,... | collective-permute-start | bytes 36872 | tf_op jit(solution)/shard_map/ppermute | solution.py:53
  150.6 3.8 %collective-permute-start.9 = (f32[3,1024]{1,0:T(4,128)S(1)}, f32[3,1024]{1,0:T(4,128)S(1)}, u32[]{:S(2)}, u32[]{:S(2)}) collective-permute-start(f32[3,1024]{1,0:T(4,128)S(1)} %pad_maximum_fusion.2), channel_id=1, source_target_pairs={{0,4},{1,5},{2,6},{3,7},{4,0},{5,1},{6,2},{7,3},{8,12},{9,13},{10,... | collective-permute-start | bytes 36872 | tf_op jit(solution)/shard_map/ppermute | solution.py:53
  154.5 5.3 %collective-permute-start.10 = (f32[3,1024]{1,0:T(4,128)S(1)}, f32[3,1024]{1,0:T(4,128)S(1)}, u32[]{:S(2)}, u32[]{:S(2)}) collective-permute-start(f32[3,1024]{1,0:T(4,128)S(1)} %pad_maximum_fusion.3), channel_id=1, source_target_pairs={{0,8},{1,9},{2,10},{3,11},{4,12},{5,13},{6,14},{7,15},{8,0},{9,1},... | collective-permute-start | bytes 36872 | tf_op jit(solution)/shard_map/ppermute | solution.py:53
  159.9 3.8 %collective-permute-start.11 = (f32[3,1024]{1,0:T(4,128)S(1)}, f32[3,1024]{1,0:T(4,128)S(1)}, u32[]{:S(2)}, u32[]{:S(2)}) collective-permute-start(f32[3,1024]{1,0:T(4,128)S(1)} %pad_maximum_fusion.4), channel_id=1, source_target_pairs={{0,16},{16,0},{32,48},{48,32},{64,80},{80,64},{96,112},{112,96},{1... | collective-permute-start | bytes 36872 | tf_op jit(solution)/shard_map/ppermute | solution.py:53
  163.8 5.3 %collective-permute-start.12 = (f32[3,1024]{1,0:T(4,128)S(1)}, f32[3,1024]{1,0:T(4,128)S(1)}, u32[]{:S(2)}, u32[]{:S(2)}) collective-permute-start(f32[3,1024]{1,0:T(4,128)S(1)} %pad_maximum_fusion.5), channel_id=1, source_target_pairs={{0,32},{16,48},{32,0},{48,16},{64,96},{80,112},{96,64},{112,80},{1... | collective-permute-start | bytes 36872 | tf_op jit(solution)/shard_map/ppermute | solution.py:53
  169.1 5.5 %collective-permute-start.13 = (f32[3,1024]{1,0:T(4,128)S(1)}, f32[3,1024]{1,0:T(4,128)S(1)}, u32[]{:S(2)}, u32[]{:S(2)}) collective-permute-start(f32[3,1024]{1,0:T(4,128)S(1)} %pad_maximum_fusion.6), channel_id=1, source_target_pairs={{0,64},{16,80},{32,96},{48,112},{64,0},{80,16},{96,32},{112,48},{1... | collective-permute-start | bytes 36872 | tf_op jit(solution)/shard_map/ppermute | solution.py:53
  174.7 20.9 %copy-start.2 = (f32[1024]{0:T(1024)}, f32[1024]{0:T(1024)S(1)}, u32[]{:S(2)}) copy-start(f32[1024]{0:T(1024)S(1)} %get-tuple-element.6) | copy-start | bytes 12292
Sparse Core Ops, SparseCore 0:
  38.8 89.5 all-gather.1
